TPU v7x, 256 devices: a whole 4x4x8 slice. The times are simulated.
256 devices in a mesh: gx: 32 (over z_hi, y, core), gy: 8 (over z_lo, x).
Axes of the slice: x: 4, y: 4, z: 8 (z_hi: 4, z_lo: 2; z = z_hi * 2 + z_lo), core: 2. Of those that a mesh axis runs over, the one named last changes fastest.
Arguments:
- state: float32 [5, 256, 64, 128], P(None, 'gx', 'gy'), may hold values from -6 to 6
- terrain: int32 [256, 64], P('gx', 'gy'), may hold values from 0 to 31
- site_cells: int32 [65536], P(('gx', 'gy')), may hold values from 0 to 8191
- site_values: float32 [5, 65536], P(None, ('gx', 'gy')), may hold values from -6 to 6
- w_in: float32 [64, 4], replicated, may hold values from -3 to 3
- b_in: float32 [64], replicated, may hold values from -3 to 3
- w_out: float32 [64], replicated, may hold values from -1.5 to 1.5
Outputs:
- state_grad: float32 [5, 256, 64, 128], P(None, 'gx', 'gy')
- closure_grad: float32 [64, 6], replicated
Inputs may be any that keep to these rules, and one draw needn't show every extreme that they name: `site_cells`: site s lies on the device that holds entry s; its id names a cell of that device's block as (i * 8 + j) * 128 + k for local position (i, j, k).
All inputs are finite; a program needn't handle non-finite values.
Results may differ from a plain program's by a relative error of at most 0.0003.
Values sent between devices are 32-bit elements; how exact they have to be, the bound alone decides.
No kernel may reach another device: no remote copies, remote signals or barrier semaphores. Data moves between devices by JAX's collectives and lax.ppermute only.
A program may use at most 128 MiB of HBM per device.

v0:
```python
import jax
import jax.numpy as jnp
from jax import lax
from jax.sharding import PartitionSpec as P

STEPS = 4
PRECISE = lax.Precision.HIGHEST


def padded_2(cells, sides, width):
    for axis, dim in sides:
        count = lax.axis_size(axis)
        ends = count - 1
        head = lax.slice_in_dim(cells, 0, width, axis=dim)
        tail = lax.slice_in_dim(cells, cells.shape[dim] - width, cells.shape[dim], axis=dim)
        cells = jnp.concatenate(
            [
                lax.ppermute(tail, axis, [(i, (i + 1) % count) for i in range(ends)]),
                cells,
                lax.ppermute(head, axis, [((i + 1) % count, i) for i in range(ends)]),
            ],
            axis=dim,
        )
    return cells


def vertical_diff(values):
    blank = jnp.zeros_like(values[..., :1])
    upper = jnp.concatenate([values[..., 1:], blank], axis=-1)
    lower = jnp.concatenate([blank, values[..., :-1]], axis=-1)
    return 0.5 * (upper - lower)


def closure_inputs(fields, terrain):
    levels = jnp.arange(fields.shape[-1], dtype=jnp.int32)
    height = 2.0 * (levels - terrain[..., None]).astype(jnp.float32) / fields.shape[-1]
    return jnp.stack(
        [vertical_diff(fields[0]), vertical_diff(fields[1]), vertical_diff(fields[2]), height]
    )


def hidden_units(inputs, w_in, b_in):
    before = jnp.einsum("hf,f...->h...", w_in, inputs, precision=PRECISE)
    return jnp.tanh(before + b_in.reshape((-1,) + (1,) * (inputs.ndim - 1)))


def viscosity(hidden, w_out):
    logit = jnp.einsum("h,h...->...", w_out, hidden, precision=PRECISE)
    return 0.16 * jax.nn.sigmoid(logit)


def interior(values):
    return values[..., 1:-1, 1:-1, :]


def beside(values):
    return [
        values[..., 2:, 1:-1, :],
        values[..., :-2, 1:-1, :],
        values[..., 1:-1, 2:, :],
        values[..., 1:-1, :-2, :],
    ]


def above_below(values):
    blank = jnp.zeros_like(values[..., :1])
    return [
        jnp.concatenate([values[..., 1:], blank], axis=-1),
        jnp.concatenate([blank, values[..., :-1]], axis=-1),
    ]


def fluid_cells(terrain, levels_count):
    levels = jnp.arange(levels_count, dtype=jnp.int32)
    return (levels >= terrain[..., None]).astype(jnp.float32)


def advance(fields, viscous, fluid):
    centre = interior(fields)
    visc_mid = interior(viscous)
    fluid_mid = interior(fluid)
    near_sets = list(zip(beside(fields), beside(viscous), beside(fluid)))
    near_sets = near_sets + list(
        zip(above_below(centre), above_below(visc_mid), above_below(fluid_mid))
    )
    summed = centre
    for field_near, visc_near, fluid_near in near_sets:
        conductance = fluid_mid * fluid_near * 0.5 * (visc_mid + visc_near)
        summed = summed + conductance * (field_near - centre)
    return summed


def adjoint_step(padded, viscous, fluid, terrain, backward, w_in, b_in, w_out):
    centre = interior(padded)
    visc_mid = interior(viscous)
    fluid_mid = interior(fluid)
    back_mid = interior(backward)
    near_sets = list(zip(beside(padded), beside(viscous), beside(fluid), beside(backward)))
    near_sets = near_sets + list(
        zip(
            above_below(centre),
            above_below(visc_mid),
            above_below(fluid_mid),
            above_below(back_mid),
        )
    )
    result = back_mid
    visc_grad = jnp.zeros(visc_mid.shape, jnp.float32)
    for field_near, visc_near, fluid_near, back_near in near_sets:
        open_face = fluid_mid * fluid_near
        conductance = open_face * 0.5 * (visc_mid + visc_near)
        result = result + conductance * (back_near - back_mid)
        visc_grad = visc_grad + open_face * 0.5 * jnp.sum(
            (field_near - centre) * (back_mid - back_near), axis=0
        )
    inputs = closure_inputs(centre, terrain[1:-1, 1:-1])
    hidden = hidden_units(inputs, w_in, b_in)
    logit = jnp.einsum("h,h...->...", w_out, hidden, precision=PRECISE)
    squash = jax.nn.sigmoid(logit)
    logit_grad = visc_grad * 0.16 * squash * (1.0 - squash)
    before_grad = w_out[:, None, None, None] * logit_grad * (1.0 - hidden * hidden)
    out_grad = jnp.einsum("...,h...->h", logit_grad, hidden, precision=PRECISE)
    in_grad = jnp.einsum("h...,f...->hf", before_grad, inputs, precision=PRECISE)
    bias_grad = jnp.sum(before_grad, axis=(1, 2, 3))
    input_grad = jnp.einsum("hf,h...->f...", w_in, before_grad, precision=PRECISE)
    result = result.at[:3].add(-vertical_diff(input_grad[:3]))
    partial_grad = jnp.concatenate([in_grad, bias_grad[:, None], out_grad[:, None]], axis=1)
    return (result, partial_grad)


def seed_from(final, site_cells, site_values):
    flat = final.reshape(final.shape[0], -1)
    misfit = flat[:, site_cells] - site_values
    return jnp.zeros_like(flat).at[:, site_cells].add(misfit).reshape(final.shape)


def add_partial(grad_sum, partial_grad):
    return grad_sum + partial_grad


def body(state, terrain, site_cells, site_values, w_in, b_in, w_out):
    fields_count, width_x, width_y, levels_count = state.shape
    top_code = levels_count - terrain
    grad_sum = jnp.zeros((w_in.shape[0], w_in.shape[1] + 2), jnp.float32)
    saved = []
    code_padded = padded_2(top_code, (("gx", 0), ("gy", 1)), 1)
    terrain_padded = levels_count - code_padded
    fluid_padded = fluid_cells(terrain_padded, levels_count)
    fields = state
    for step_index in range(STEPS):
        padded = padded_2(fields, (("gx", 1), ("gy", 2)), 1)
        viscous = viscosity(hidden_units(closure_inputs(padded, terrain_padded), w_in, b_in), w_out)
        saved.append((padded, viscous, fluid_padded, terrain_padded))
        fields = advance(padded, viscous, fluid_padded)
    backward = seed_from(fields, site_cells, site_values)
    for step_index in range(STEPS - 1, -1, -1):
        padded, viscous, fluid_padded, terrain_padded = saved[step_index]
        back_padded = padded_2(backward, (("gx", 1), ("gy", 2)), 1)
        backward, partial_grad = adjoint_step(
            padded, viscous, fluid_padded, terrain_padded, back_padded, w_in, b_in, w_out
        )
        grad_sum = add_partial(grad_sum, partial_grad)
    closure_sum = lax.psum(grad_sum, ("gx", "gy"))
    site_total = site_cells.shape[0] * lax.axis_size("gx") * lax.axis_size("gy")
    return (backward, closure_sum * site_total ** (-0.5))


def solution(mesh):
    return jax.shard_map(
        body,
        mesh=mesh,
        in_specs=(
            P(None, "gx", "gy", None),
            P("gx", "gy"),
            P(("gx", "gy")),
            P(None, ("gx", "gy")),
            P(),
            P(),
            P(),
        ),
        out_specs=(P(None, "gx", "gy", None), P()),
        check_vma=False,
    )
```

profile of v0, /device:TPU:1, one launch (start us, length us, event | category | flops | bytes accessed | tf_op | source)
XLA Modules:
  0.0 348.7 jit_solution(16706777080903427037)
XLA Ops:
  1.5 4.6 %collective-permute-start.4 = (f32[5,1,8,128]{3,2,1,0:T(8,128)S(1)}, f32[5,1,8,128]{3,2,1,0:T(8,128)S(1)}, u32[]{:S(2)}, u32[]{:S(2)}) collective-permute-start(f32[5,1,8,128]{3,2,1,0:T(8,128)S(1)} %get-tuple-element.168), channel_id=1, source_target_pairs={{0,8},{8,16},{16,24},{24,32},{32,40},{40,48},{48,56},{56,64},{64,7... | collective-permute-start | bytes 61448 | tf_op jit(solution)/shard_map/ppermute | solution.py:18
  6.0 1.9 collective-permute-start.5
  8.7 3.6 %collective-permute-start = (s32[1,8]{1,0:T(1,128)S(1)}, s32[1,8]{1,0:T(1,128)S(1)}, u32[]{:S(2)}, u32[]{:S(2)}) collective-permute-start(s32[1,8]{1,0:T(1,128)S(1)} %get-tuple-element.260), channel_id=1, source_target_pairs={{0,8},{8,16},{16,24},{24,32},{32,40},{40,48},{48,56},{56,64},{64,7... | collective-permute-start | bytes 104 | tf_op jit(solution)/shard_map/ppermute | solution.py:18
  12.3 1.9 collective-permute-start.1
  18.9 3.1 collective-permute-start.2
  23.3 3.1 collective-permute-done.3
  26.9 3.1 collective-permute-start.6
  31.5 3.2 collective-permute-done.7
  35.3 2.8 fusion.104
  38.1 2.1 fusion.6
  40.9 6.5 %collective-permute-start.8 = (f32[5,1,8,128]{3,2,1,0:T(8,128)S(1)}, f32[5,1,8,128]{3,2,1,0:T(8,128)S(1)}, u32[]{:S(2)}, u32[]{:S(2)}) collective-permute-start(f32[5,1,8,128]{3,2,1,0:T(8,128)S(1)} %get-tuple-element.156), channel_id=1, source_target_pairs={{0,8},{8,16},{16,24},{24,32},{32,40},{40,48},{48,56},{56,64},{64,7... | collective-permute-start | bytes 61448 | tf_op jit(solution)/shard_map/ppermute | solution.py:18
  49.7 2.8 collective-permute-done.9
  52.5 4.8 %collective-permute-start.10 = (f32[5,10,1,128]{3,2,1,0:T(1,128)S(1)}, f32[5,10,1,128]{3,2,1,0:T(1,128)S(1)}, u32[]{:S(2)}, u32[]{:S(2)}) collective-permute-start(f32[5,10,1,128]{3,2,1,0:T(1,128)S(1)} %get-tuple-element.114), channel_id=1, source_target_pairs={{0,1},{1,2},{2,3},{3,4},{4,5},{5,6},{6,7},{8,9},{9,10},{10,11},{11... | collective-permute-start | bytes 76808 | tf_op jit(solution)/shard_map/ppermute | solution.py:18
  58.9 3.3 collective-permute-done.11
  62.8 2.8 fusion.102
  65.6 2.1 fusion.4
  68.7 3.1 collective-permute-start.12
  74.1 2.8 collective-permute-done.13
  76.9 3.7 %collective-permute-start.14 = (f32[5,10,1,128]{3,2,1,0:T(1,128)S(1)}, f32[5,10,1,128]{3,2,1,0:T(1,128)S(1)}, u32[]{:S(2)}, u32[]{:S(2)}) collective-permute-start(f32[5,10,1,128]{3,2,1,0:T(1,128)S(1)} %get-tuple-element.112), channel_id=1, source_target_pairs={{0,1},{1,2},{2,3},{3,4},{4,5},{5,6},{6,7},{8,9},{9,10},{10,11},{11... | collective-permute-start | bytes 76808 | tf_op jit(solution)/shard_map/ppermute | solution.py:18
  82.1 3.5 collective-permute-done.15
  86.2 2.8 fusion.100
  89.0 2.1 fusion.2
  91.6 3.1 collective-permute-start.16
  94.7 2.3 collective-permute-start.17
  112.6 3.7 %collective-permute-start.18 = (f32[5,10,1,128]{3,2,1,0:T(1,128)S(1)}, f32[5,10,1,128]{3,2,1,0:T(1,128)S(1)}, u32[]{:S(2)}, u32[]{:S(2)}) collective-permute-start(f32[5,10,1,128]{3,2,1,0:T(1,128)S(1)} %get-tuple-element.110), channel_id=1, source_target_pairs={{0,1},{1,2},{2,3},{3,4},{4,5},{5,6},{6,7},{8,9},{9,10},{10,11},{11... | collective-permute-start | bytes 76808 | tf_op jit(solution)/shard_map/ppermute | solution.py:18
  118.0 3.2 collective-permute-done.19
  121.9 2.8 fusion.98
  124.7 2.1 fusion
  127.8 2.7 copy.93
  130.5 5.8 %scatter_custom_fusion = f32[5,8192]{0,1:T(8,128)} fusion(s32[256]{0:T(256)} %copy-done.109, f32[]{:T(128)} %constant.113.clone.1, f32[5,256]{0,1:T(8,128)} %copy.50, f32[5,8192]{0,1:T(8,128)} %bitcast.362, s32[1024]{0:T(1024)S(1)} %pad_clamp_fusion), kind=kCustom, calls=%fused_computation.50 | custom fusion | flops 2560 | bytes 4493824 | tf_op jit(solution)/shard_map/scatter-add | solution.py:134
  136.3 2.9 copy.94
  139.3 2.1 collective-permute-start.20
  141.3 4.8 %collective-permute-start.21 = (f32[5,1,8,128]{3,2,1,0:T(8,128)S(1)}, f32[5,1,8,128]{3,2,1,0:T(8,128)S(1)}, u32[]{:S(2)}, u32[]{:S(2)}) collective-permute-start(f32[5,1,8,128]{3,2,1,0:T(8,128)S(1)} %get-tuple-element.144), channel_id=1, source_target_pairs={{0,8},{8,16},{16,24},{24,32},{32,40},{40,48},{48,56},{56,64},{64,7... | collective-permute-start | bytes 61448 | tf_op jit(solution)/shard_map/ppermute | solution.py:18
  148.4 4.6 %collective-permute-start.23 = (f32[5,10,1,128]{3,2,1,0:T(1,128)S(1)}, f32[5,10,1,128]{3,2,1,0:T(1,128)S(1)}, u32[]{:S(2)}, u32[]{:S(2)}) collective-permute-start(f32[5,10,1,128]{3,2,1,0:T(1,128)S(1)} %get-tuple-element.109), channel_id=1, source_target_pairs={{0,1},{1,2},{2,3},{3,4},{4,5},{5,6},{6,7},{8,9},{9,10},{10,11},{11... | collective-permute-start | bytes 76808 | tf_op jit(solution)/shard_map/ppermute | solution.py:18
  157.0 2.0 convolution_bitcast_fusion.3
  159.0 2.1 collective-permute-start.24
  161.0 6.4 %collective-permute-start.25 = (f32[5,1,8,128]{3,2,1,0:T(8,128)S(1)}, f32[5,1,8,128]{3,2,1,0:T(8,128)S(1)}, u32[]{:S(2)}, u32[]{:S(2)}) collective-permute-start(f32[5,1,8,128]{3,2,1,0:T(8,128)S(1)} %get-tuple-element.137), channel_id=1, source_target_pairs={{0,8},{8,16},{16,24},{24,32},{32,40},{40,48},{48,56},{56,64},{64,7... | collective-permute-start | bytes 61448 | tf_op jit(solution)/shard_map/ppermute | solution.py:18
  170.5 4.6 %collective-permute-start.27 = (f32[5,10,1,128]{3,2,1,0:T(1,128)S(1)}, f32[5,10,1,128]{3,2,1,0:T(1,128)S(1)}, u32[]{:S(2)}, u32[]{:S(2)}) collective-permute-start(f32[5,10,1,128]{3,2,1,0:T(1,128)S(1)} %get-tuple-element.107), channel_id=1, source_target_pairs={{0,1},{1,2},{2,3},{3,4},{4,5},{5,6},{6,7},{8,9},{9,10},{10,11},{11... | collective-permute-start | bytes 76808 | tf_op jit(solution)/shard_map/ppermute | solution.py:18
  178.8 2.0 convolution_bitcast_fusion.2
  180.8 2.1 collective-permute-start.28
  182.8 7.3 %collective-permute-start.29 = (f32[5,1,8,128]{3,2,1,0:T(8,128)S(1)}, f32[5,1,8,128]{3,2,1,0:T(8,128)S(1)}, u32[]{:S(2)}, u32[]{:S(2)}) collective-permute-start(f32[5,1,8,128]{3,2,1,0:T(8,128)S(1)} %get-tuple-element.130), channel_id=1, source_target_pairs={{0,8},{8,16},{16,24},{24,32},{32,40},{40,48},{48,56},{56,64},{64,7... | collective-permute-start | bytes 61448 | tf_op jit(solution)/shard_map/ppermute | solution.py:18
  193.3 4.8 %collective-permute-start.31 = (f32[5,10,1,128]{3,2,1,0:T(1,128)S(1)}, f32[5,10,1,128]{3,2,1,0:T(1,128)S(1)}, u32[]{:S(2)}, u32[]{:S(2)}) collective-permute-start(f32[5,10,1,128]{3,2,1,0:T(1,128)S(1)} %get-tuple-element.105), channel_id=1, source_target_pairs={{0,1},{1,2},{2,3},{3,4},{4,5},{5,6},{6,7},{8,9},{9,10},{10,11},{11... | collective-permute-start | bytes 76808 | tf_op jit(solution)/shard_map/ppermute | solution.py:18
  201.5 2.0 convolution_bitcast_fusion.1
  203.5 2.1 collective-permute-start.32
  205.6 4.5 %collective-permute-start.33 = (f32[5,1,8,128]{3,2,1,0:T(8,128)S(1)}, f32[5,1,8,128]{3,2,1,0:T(8,128)S(1)}, u32[]{:S(2)}, u32[]{:S(2)}) collective-permute-start(f32[5,1,8,128]{3,2,1,0:T(8,128)S(1)} %get-tuple-element.123), channel_id=1, source_target_pairs={{0,8},{8,16},{16,24},{24,32},{32,40},{40,48},{48,56},{56,64},{64,7... | collective-permute-start | bytes 61448 | tf_op jit(solution)/shard_map/ppermute | solution.py:18
  213.2 6.2 %collective-permute-start.35 = (f32[5,10,1,128]{3,2,1,0:T(1,128)S(1)}, f32[5,10,1,128]{3,2,1,0:T(1,128)S(1)}, u32[]{:S(2)}, u32[]{:S(2)}) collective-permute-start(f32[5,10,1,128]{3,2,1,0:T(1,128)S(1)} %get-tuple-element.103), channel_id=1, source_target_pairs={{0,1},{1,2},{2,3},{3,4},{4,5},{5,6},{6,7},{8,9},{9,10},{10,11},{11... | collective-permute-start | bytes 76808 | tf_op jit(solution)/shard_map/ppermute | solution.py:18
  220.6 2.0 convolution_bitcast_fusion
  227.6 118.9 %psum.7 = f32[64,6]{0,1:T(8,128)S(1)} all-reduce(f32[64,6]{0,1:T(8,128)S(1)} %fusion.281), channel_id=1, replica_groups=mesh['gx'=32,'gy'=8] {'gx','gy'}, use_global_device_ids=true, to_apply=%region_29.0 | all-reduce | flops 384 | bytes 3072 | tf_op jit(solution)/shard_map/psum | solution.py:163
  (423 shorter events, 68.8 us)
Async XLA Ops:
  0.6 34.6 %copy-start = (f32[64,4]{0,1:T(4,128)S(1)}, f32[64,4]{0,1:T(4,128)}, u32[]{:S(2)}) copy-start(f32[64,4]{0,1:T(4,128)} %param.19) | copy-start | bytes 3076
  0.6 26.2 %copy-start.7 = (f32[5,8,8,128]{3,2,1,0:T(8,128)S(1)}, f32[5,8,8,128]{3,2,1,0:T(8,128)}, u32[]{:S(2)}) copy-start(f32[5,8,8,128]{3,2,1,0:T(8,128)} %param.15) | copy-start | bytes 491524
  1.5 25.4 %collective-permute-start.4 = (f32[5,1,8,128]{3,2,1,0:T(8,128)S(1)}, f32[5,1,8,128]{3,2,1,0:T(8,128)S(1)}, u32[]{:S(2)}, u32[]{:S(2)}) collective-permute-start(f32[5,1,8,128]{3,2,1,0:T(8,128)S(1)} %get-tuple-element.168), channel_id=1, source_target_pairs={{0,8},{8,16},{16,24},{24,32},{32,40},{40,48},{48,56},{56,64},{64,7... | collective-permute-start | bytes 61448 | tf_op jit(solution)/shard_map/ppermute | solution.py:18
  6.0 20.8 %collective-permute-start.5 = (f32[5,1,8,128]{3,2,1,0:T(8,128)S(1)}, f32[5,1,8,128]{3,2,1,0:T(8,128)S(1)}, u32[]{:S(2)}, u32[]{:S(2)}) collective-permute-start(f32[5,1,8,128]{3,2,1,0:T(8,128)S(1)} %get-tuple-element.169), channel_id=1, source_target_pairs={{8,0},{16,8},{24,16},{32,24},{40,32},{48,40},{56,48},{64,56},{72,6... | collective-permute-start | bytes 61448 | tf_op jit(solution)/shard_map/ppermute | solution.py:20
  8.7 10.1 %collective-permute-start = (s32[1,8]{1,0:T(1,128)S(1)}, s32[1,8]{1,0:T(1,128)S(1)}, u32[]{:S(2)}, u32[]{:S(2)}) collective-permute-start(s32[1,8]{1,0:T(1,128)S(1)} %get-tuple-element.260), channel_id=1, source_target_pairs={{0,8},{8,16},{16,24},{24,32},{32,40},{40,48},{48,56},{56,64},{64,7... | collective-permute-start | bytes 104 | tf_op jit(solution)/shard_map/ppermute | solution.py:18
  12.3 6.5 %collective-permute-start.1 = (s32[1,8]{1,0:T(1,128)S(1)}, s32[1,8]{1,0:T(1,128)S(1)}, u32[]{:S(2)}, u32[]{:S(2)}) collective-permute-start(s32[1,8]{1,0:T(1,128)S(1)} %get-tuple-element.261), channel_id=1, source_target_pairs={{8,0},{16,8},{24,16},{32,24},{40,32},{48,40},{56,48},{64,56},{72,6... | collective-permute-start | bytes 104 | tf_op jit(solution)/shard_map/ppermute | solution.py:20
  15.3 25.1 %copy-start.8 = (f32[5,8,8,127]{3,2,1,0:T(8,128)}, f32[5,8,8,127]{3,2,1,0:T(8,128)S(1)}, u32[]{:S(2)}) copy-start(f32[5,8,8,127]{3,2,1,0:T(8,128)S(1)} %get-tuple-element.159) | copy-start | bytes 487684
  18.9 4.4 %collective-permute-start.2 = (s32[10,1]{1,0:T(8,128)S(1)}, s32[10,1]{1,0:T(8,128)S(1)}, u32[]{:S(2)}, u32[]{:S(2)}) collective-permute-start(s32[10,1]{1,0:T(8,128)S(1)} %get-tuple-element.258), channel_id=1, source_target_pairs={{0,1},{1,2},{2,3},{3,4},{4,5},{5,6},{6,7},{8,9},{9,10},{10,11},{11... | collective-permute-start | bytes 128 | tf_op jit(solution)/shard_map/ppermute | solution.py:18
  22.0 4.4 %collective-permute-start.3 = (s32[10,1]{1,0:T(8,128)S(1)}, s32[10,1]{1,0:T(8,128)S(1)}, u32[]{:S(2)}, u32[]{:S(2)}) collective-permute-start(s32[10,1]{1,0:T(8,128)S(1)} %get-tuple-element.259), channel_id=1, source_target_pairs={{1,0},{2,1},{3,2},{4,3},{5,4},{6,5},{7,6},{9,8},{10,9},{11,10},{12... | collective-permute-start | bytes 128 | tf_op jit(solution)/shard_map/ppermute | solution.py:20
  26.9 4.5 %collective-permute-start.6 = (f32[5,10,1,128]{3,2,1,0:T(1,128)S(1)}, f32[5,10,1,128]{3,2,1,0:T(1,128)S(1)}, u32[]{:S(2)}, u32[]{:S(2)}) collective-permute-start(f32[5,10,1,128]{3,2,1,0:T(1,128)S(1)} %get-tuple-element.116), channel_id=1, source_target_pairs={{0,1},{1,2},{2,3},{3,4},{4,5},{5,6},{6,7},{8,9},{9,10},{10,11},{11... | collective-permute-start | bytes 76808 | tf_op jit(solution)/shard_map/ppermute | solution.py:18
  30.1 4.6 %collective-permute-start.7 = (f32[5,10,1,128]{3,2,1,0:T(1,128)S(1)}, f32[5,10,1,128]{3,2,1,0:T(1,128)S(1)}, u32[]{:S(2)}, u32[]{:S(2)}) collective-permute-start(f32[5,10,1,128]{3,2,1,0:T(1,128)S(1)} %get-tuple-element.117), channel_id=1, source_target_pairs={{1,0},{2,1},{3,2},{4,3},{5,4},{6,5},{7,6},{9,8},{10,9},{11,10},{12... | collective-permute-start | bytes 76808 | tf_op jit(solution)/shard_map/ppermute | solution.py:20
  40.8 27.1 %copy-start.10 = (f32[5,8,8,127]{3,2,1,0:T(8,128)}, f32[5,8,8,127]{3,2,1,0:T(8,128)S(1)}, u32[]{:S(2)}) copy-start(f32[5,8,8,127]{3,2,1,0:T(8,128)S(1)} %get-tuple-element.154) | copy-start | bytes 487684
  40.8 27.1 %copy-start.12 = (f32[5,8,8,127]{3,2,1,0:T(8,128)}, f32[5,8,8,127]{3,2,1,0:T(8,128)S(1)}, u32[]{:S(2)}) copy-start(f32[5,8,8,127]{3,2,1,0:T(8,128)S(1)} %get-tuple-element.155) | copy-start | bytes 487684
  40.9 8.8 %collective-permute-start.8 = (f32[5,1,8,128]{3,2,1,0:T(8,128)S(1)}, f32[5,1,8,128]{3,2,1,0:T(8,128)S(1)}, u32[]{:S(2)}, u32[]{:S(2)}) collective-permute-start(f32[5,1,8,128]{3,2,1,0:T(8,128)S(1)} %get-tuple-element.156), channel_id=1, source_target_pairs={{0,8},{8,16},{16,24},{24,32},{32,40},{40,48},{48,56},{56,64},{64,7... | collective-permute-start | bytes 61448 | tf_op jit(solution)/shard_map/ppermute | solution.py:18
  47.4 5.1 %collective-permute-start.9 = (f32[5,1,8,128]{3,2,1,0:T(8,128)S(1)}, f32[5,1,8,128]{3,2,1,0:T(8,128)S(1)}, u32[]{:S(2)}, u32[]{:S(2)}) collective-permute-start(f32[5,1,8,128]{3,2,1,0:T(8,128)S(1)} %get-tuple-element.157), channel_id=1, source_target_pairs={{8,0},{16,8},{24,16},{32,24},{40,32},{48,40},{56,48},{64,56},{72,6... | collective-permute-start | bytes 61448 | tf_op jit(solution)/shard_map/ppermute | solution.py:20
  52.5 6.4 %collective-permute-start.10 = (f32[5,10,1,128]{3,2,1,0:T(1,128)S(1)}, f32[5,10,1,128]{3,2,1,0:T(1,128)S(1)}, u32[]{:S(2)}, u32[]{:S(2)}) collective-permute-start(f32[5,10,1,128]{3,2,1,0:T(1,128)S(1)} %get-tuple-element.114), channel_id=1, source_target_pairs={{0,1},{1,2},{2,3},{3,4},{4,5},{5,6},{6,7},{8,9},{9,10},{10,11},{11... | collective-permute-start | bytes 76808 | tf_op jit(solution)/shard_map/ppermute | solution.py:18
  57.3 4.9 %collective-permute-start.11 = (f32[5,10,1,128]{3,2,1,0:T(1,128)S(1)}, f32[5,10,1,128]{3,2,1,0:T(1,128)S(1)}, u32[]{:S(2)}, u32[]{:S(2)}) collective-permute-start(f32[5,10,1,128]{3,2,1,0:T(1,128)S(1)} %get-tuple-element.115), channel_id=1, source_target_pairs={{1,0},{2,1},{3,2},{4,3},{5,4},{6,5},{7,6},{9,8},{10,9},{11,10},{12... | collective-permute-start | bytes 76808 | tf_op jit(solution)/shard_map/ppermute | solution.py:20
  68.7 22.7 %copy-start.14 = (f32[5,8,8,127]{3,2,1,0:T(8,128)}, f32[5,8,8,127]{3,2,1,0:T(8,128)S(1)}, u32[]{:S(2)}) copy-start(f32[5,8,8,127]{3,2,1,0:T(8,128)S(1)} %get-tuple-element.150) | copy-start | bytes 487684
  68.7 5.4 %collective-permute-start.12 = (f32[5,1,8,128]{3,2,1,0:T(8,128)S(1)}, f32[5,1,8,128]{3,2,1,0:T(8,128)S(1)}, u32[]{:S(2)}, u32[]{:S(2)}) collective-permute-start(f32[5,1,8,128]{3,2,1,0:T(8,128)S(1)} %get-tuple-element.152), channel_id=1, source_target_pairs={{0,8},{8,16},{16,24},{24,32},{32,40},{40,48},{48,56},{56,64},{64,7... | collective-permute-start | bytes 61448 | tf_op jit(solution)/shard_map/ppermute | solution.py:18
  71.8 5.1 %collective-permute-start.13 = (f32[5,1,8,128]{3,2,1,0:T(8,128)S(1)}, f32[5,1,8,128]{3,2,1,0:T(8,128)S(1)}, u32[]{:S(2)}, u32[]{:S(2)}) collective-permute-start(f32[5,1,8,128]{3,2,1,0:T(8,128)S(1)} %get-tuple-element.153), channel_id=1, source_target_pairs={{8,0},{16,8},{24,16},{32,24},{40,32},{48,40},{56,48},{64,56},{72,6... | collective-permute-start | bytes 61448 | tf_op jit(solution)/shard_map/ppermute | solution.py:20
  76.9 5.1 %collective-permute-start.14 = (f32[5,10,1,128]{3,2,1,0:T(1,128)S(1)}, f32[5,10,1,128]{3,2,1,0:T(1,128)S(1)}, u32[]{:S(2)}, u32[]{:S(2)}) collective-permute-start(f32[5,10,1,128]{3,2,1,0:T(1,128)S(1)} %get-tuple-element.112), channel_id=1, source_target_pairs={{0,1},{1,2},{2,3},{3,4},{4,5},{5,6},{6,7},{8,9},{9,10},{10,11},{11... | collective-permute-start | bytes 76808 | tf_op jit(solution)/shard_map/ppermute | solution.py:18
  80.7 4.9 %collective-permute-start.15 = (f32[5,10,1,128]{3,2,1,0:T(1,128)S(1)}, f32[5,10,1,128]{3,2,1,0:T(1,128)S(1)}, u32[]{:S(2)}, u32[]{:S(2)}) collective-permute-start(f32[5,10,1,128]{3,2,1,0:T(1,128)S(1)} %get-tuple-element.113), channel_id=1, source_target_pairs={{1,0},{2,1},{3,2},{4,3},{5,4},{6,5},{7,6},{9,8},{10,9},{11,10},{12... | collective-permute-start | bytes 76808 | tf_op jit(solution)/shard_map/ppermute | solution.py:20
  91.6 20.9 %collective-permute-start.16 = (f32[5,1,8,128]{3,2,1,0:T(8,128)S(1)}, f32[5,1,8,128]{3,2,1,0:T(8,128)S(1)}, u32[]{:S(2)}, u32[]{:S(2)}) collective-permute-start(f32[5,1,8,128]{3,2,1,0:T(8,128)S(1)} %get-tuple-element.148), channel_id=1, source_target_pairs={{0,8},{8,16},{16,24},{24,32},{32,40},{40,48},{48,56},{56,64},{64,7... | collective-permute-start | bytes 61448 | tf_op jit(solution)/shard_map/ppermute | solution.py:18
  94.7 17.9 %collective-permute-start.17 = (f32[5,1,8,128]{3,2,1,0:T(8,128)S(1)}, f32[5,1,8,128]{3,2,1,0:T(8,128)S(1)}, u32[]{:S(2)}, u32[]{:S(2)}) collective-permute-start(f32[5,1,8,128]{3,2,1,0:T(8,128)S(1)} %get-tuple-element.149), channel_id=1, source_target_pairs={{8,0},{16,8},{24,16},{32,24},{40,32},{48,40},{56,48},{64,56},{72,6... | collective-permute-start | bytes 61448 | tf_op jit(solution)/shard_map/ppermute | solution.py:20
  112.6 5.4 %collective-permute-start.18 = (f32[5,10,1,128]{3,2,1,0:T(1,128)S(1)}, f32[5,10,1,128]{3,2,1,0:T(1,128)S(1)}, u32[]{:S(2)}, u32[]{:S(2)}) collective-permute-start(f32[5,10,1,128]{3,2,1,0:T(1,128)S(1)} %get-tuple-element.110), channel_id=1, source_target_pairs={{0,1},{1,2},{2,3},{3,4},{4,5},{5,6},{6,7},{8,9},{9,10},{10,11},{11... | collective-permute-start | bytes 76808 | tf_op jit(solution)/shard_map/ppermute | solution.py:18
  116.4 4.9 %collective-permute-start.19 = (f32[5,10,1,128]{3,2,1,0:T(1,128)S(1)}, f32[5,10,1,128]{3,2,1,0:T(1,128)S(1)}, u32[]{:S(2)}, u32[]{:S(2)}) collective-permute-start(f32[5,10,1,128]{3,2,1,0:T(1,128)S(1)} %get-tuple-element.111), channel_id=1, source_target_pairs={{1,0},{2,1},{3,2},{4,3},{5,4},{6,5},{7,6},{9,8},{10,9},{11,10},{12... | collective-permute-start | bytes 76808 | tf_op jit(solution)/shard_map/ppermute | solution.py:20
  139.3 7.0 %collective-permute-start.20 = (f32[5,1,8,128]{3,2,1,0:T(8,128)S(1)}, f32[5,1,8,128]{3,2,1,0:T(8,128)S(1)}, u32[]{:S(2)}, u32[]{:S(2)}) collective-permute-start(f32[5,1,8,128]{3,2,1,0:T(8,128)S(1)} %get-tuple-element.145), channel_id=1, source_target_pairs={{8,0},{16,8},{24,16},{32,24},{40,32},{48,40},{56,48},{64,56},{72,6... | collective-permute-start | bytes 61448 | tf_op jit(solution)/shard_map/ppermute | solution.py:20
  141.3 5.7 %collective-permute-start.21 = (f32[5,1,8,128]{3,2,1,0:T(8,128)S(1)}, f32[5,1,8,128]{3,2,1,0:T(8,128)S(1)}, u32[]{:S(2)}, u32[]{:S(2)}) collective-permute-start(f32[5,1,8,128]{3,2,1,0:T(8,128)S(1)} %get-tuple-element.144), channel_id=1, source_target_pairs={{0,8},{8,16},{16,24},{24,32},{32,40},{40,48},{48,56},{56,64},{64,7... | collective-permute-start | bytes 61448 | tf_op jit(solution)/shard_map/ppermute | solution.py:18
  147.1 7.1 %collective-permute-start.22 = (f32[5,10,1,128]{3,2,1,0:T(1,128)S(1)}, f32[5,10,1,128]{3,2,1,0:T(1,128)S(1)}, u32[]{:S(2)}, u32[]{:S(2)}) collective-permute-start(f32[5,10,1,128]{3,2,1,0:T(1,128)S(1)} %get-tuple-element.108), channel_id=1, source_target_pairs={{1,0},{2,1},{3,2},{4,3},{5,4},{6,5},{7,6},{9,8},{10,9},{11,10},{12... | collective-permute-start | bytes 76808 | tf_op jit(solution)/shard_map/ppermute | solution.py:20
  148.4 5.8 %collective-permute-start.23 = (f32[5,10,1,128]{3,2,1,0:T(1,128)S(1)}, f32[5,10,1,128]{3,2,1,0:T(1,128)S(1)}, u32[]{:S(2)}, u32[]{:S(2)}) collective-permute-start(f32[5,10,1,128]{3,2,1,0:T(1,128)S(1)} %get-tuple-element.109), channel_id=1, source_target_pairs={{0,1},{1,2},{2,3},{3,4},{4,5},{5,6},{6,7},{8,9},{9,10},{10,11},{11... | collective-permute-start | bytes 76808 | tf_op jit(solution)/shard_map/ppermute | solution.py:18
  159.0 10.2 %collective-permute-start.24 = (f32[5,1,8,128]{3,2,1,0:T(8,128)S(1)}, f32[5,1,8,128]{3,2,1,0:T(8,128)S(1)}, u32[]{:S(2)}, u32[]{:S(2)}) collective-permute-start(f32[5,1,8,128]{3,2,1,0:T(8,128)S(1)} %get-tuple-element.138), channel_id=1, source_target_pairs={{8,0},{16,8},{24,16},{32,24},{40,32},{48,40},{56,48},{64,56},{72,6... | collective-permute-start | bytes 61448 | tf_op jit(solution)/shard_map/ppermute | solution.py:20
  161.0 8.1 %collective-permute-start.25 = (f32[5,1,8,128]{3,2,1,0:T(8,128)S(1)}, f32[5,1,8,128]{3,2,1,0:T(8,128)S(1)}, u32[]{:S(2)}, u32[]{:S(2)}) collective-permute-start(f32[5,1,8,128]{3,2,1,0:T(8,128)S(1)} %get-tuple-element.137), channel_id=1, source_target_pairs={{0,8},{8,16},{16,24},{24,32},{32,40},{40,48},{48,56},{56,64},{64,7... | collective-permute-start | bytes 61448 | tf_op jit(solution)/shard_map/ppermute | solution.py:18
  169.2 6.1 %collective-permute-start.26 = (f32[5,10,1,128]{3,2,1,0:T(1,128)S(1)}, f32[5,10,1,128]{3,2,1,0:T(1,128)S(1)}, u32[]{:S(2)}, u32[]{:S(2)}) collective-permute-start(f32[5,10,1,128]{3,2,1,0:T(1,128)S(1)} %get-tuple-element.106), channel_id=1, source_target_pairs={{1,0},{2,1},{3,2},{4,3},{5,4},{6,5},{7,6},{9,8},{10,9},{11,10},{12... | collective-permute-start | bytes 76808 | tf_op jit(solution)/shard_map/ppermute | solution.py:20
  170.5 5.5 %collective-permute-start.27 = (f32[5,10,1,128]{3,2,1,0:T(1,128)S(1)}, f32[5,10,1,128]{3,2,1,0:T(1,128)S(1)}, u32[]{:S(2)}, u32[]{:S(2)}) collective-permute-start(f32[5,10,1,128]{3,2,1,0:T(1,128)S(1)} %get-tuple-element.107), channel_id=1, source_target_pairs={{0,1},{1,2},{2,3},{3,4},{4,5},{5,6},{6,7},{8,9},{9,10},{10,11},{11... | collective-permute-start | bytes 76808 | tf_op jit(solution)/shard_map/ppermute | solution.py:18
  180.8 11.2 %collective-permute-start.28 = (f32[5,1,8,128]{3,2,1,0:T(8,128)S(1)}, f32[5,1,8,128]{3,2,1,0:T(8,128)S(1)}, u32[]{:S(2)}, u32[]{:S(2)}) collective-permute-start(f32[5,1,8,128]{3,2,1,0:T(8,128)S(1)} %get-tuple-element.131), channel_id=1, source_target_pairs={{8,0},{16,8},{24,16},{32,24},{40,32},{48,40},{56,48},{64,56},{72,6... | collective-permute-start | bytes 61448 | tf_op jit(solution)/shard_map/ppermute | solution.py:20
  182.8 9.1 %collective-permute-start.29 = (f32[5,1,8,128]{3,2,1,0:T(8,128)S(1)}, f32[5,1,8,128]{3,2,1,0:T(8,128)S(1)}, u32[]{:S(2)}, u32[]{:S(2)}) collective-permute-start(f32[5,1,8,128]{3,2,1,0:T(8,128)S(1)} %get-tuple-element.130), channel_id=1, source_target_pairs={{0,8},{8,16},{16,24},{24,32},{32,40},{40,48},{48,56},{56,64},{64,7... | collective-permute-start | bytes 61448 | tf_op jit(solution)/shard_map/ppermute | solution.py:18
  192.0 6.3 %collective-permute-start.30 = (f32[5,10,1,128]{3,2,1,0:T(1,128)S(1)}, f32[5,10,1,128]{3,2,1,0:T(1,128)S(1)}, u32[]{:S(2)}, u32[]{:S(2)}) collective-permute-start(f32[5,10,1,128]{3,2,1,0:T(1,128)S(1)} %get-tuple-element.104), channel_id=1, source_target_pairs={{1,0},{2,1},{3,2},{4,3},{5,4},{6,5},{7,6},{9,8},{10,9},{11,10},{12... | collective-permute-start | bytes 76808 | tf_op jit(solution)/shard_map/ppermute | solution.py:20
  193.3 5.5 %collective-permute-start.31 = (f32[5,10,1,128]{3,2,1,0:T(1,128)S(1)}, f32[5,10,1,128]{3,2,1,0:T(1,128)S(1)}, u32[]{:S(2)}, u32[]{:S(2)}) collective-permute-start(f32[5,10,1,128]{3,2,1,0:T(1,128)S(1)} %get-tuple-element.105), channel_id=1, source_target_pairs={{0,1},{1,2},{2,3},{3,4},{4,5},{5,6},{6,7},{8,9},{9,10},{10,11},{11... | collective-permute-start | bytes 76808 | tf_op jit(solution)/shard_map/ppermute | solution.py:18
  203.5 8.4 %collective-permute-start.32 = (f32[5,1,8,128]{3,2,1,0:T(8,128)S(1)}, f32[5,1,8,128]{3,2,1,0:T(8,128)S(1)}, u32[]{:S(2)}, u32[]{:S(2)}) collective-permute-start(f32[5,1,8,128]{3,2,1,0:T(8,128)S(1)} %get-tuple-element.124), channel_id=1, source_target_pairs={{8,0},{16,8},{24,16},{32,24},{40,32},{48,40},{56,48},{64,56},{72,6... | collective-permute-start | bytes 61448 | tf_op jit(solution)/shard_map/ppermute | solution.py:20
  205.6 6.3 %collective-permute-start.33 = (f32[5,1,8,128]{3,2,1,0:T(8,128)S(1)}, f32[5,1,8,128]{3,2,1,0:T(8,128)S(1)}, u32[]{:S(2)}, u32[]{:S(2)}) collective-permute-start(f32[5,1,8,128]{3,2,1,0:T(8,128)S(1)} %get-tuple-element.123), channel_id=1, source_target_pairs={{0,8},{8,16},{16,24},{24,32},{32,40},{40,48},{48,56},{56,64},{64,7... | collective-permute-start | bytes 61448 | tf_op jit(solution)/shard_map/ppermute | solution.py:18
  211.9 7.7 %collective-permute-start.34 = (f32[5,10,1,128]{3,2,1,0:T(1,128)S(1)}, f32[5,10,1,128]{3,2,1,0:T(1,128)S(1)}, u32[]{:S(2)}, u32[]{:S(2)}) collective-permute-start(f32[5,10,1,128]{3,2,1,0:T(1,128)S(1)} %get-tuple-element.102), channel_id=1, source_target_pairs={{1,0},{2,1},{3,2},{4,3},{5,4},{6,5},{7,6},{9,8},{10,9},{11,10},{12... | collective-permute-start | bytes 76808 | tf_op jit(solution)/shard_map/ppermute | solution.py:20
  213.2 7.2 %collective-permute-start.35 = (f32[5,10,1,128]{3,2,1,0:T(1,128)S(1)}, f32[5,10,1,128]{3,2,1,0:T(1,128)S(1)}, u32[]{:S(2)}, u32[]{:S(2)}) collective-permute-start(f32[5,10,1,128]{3,2,1,0:T(1,128)S(1)} %get-tuple-element.103), channel_id=1, source_target_pairs={{0,1},{1,2},{2,3},{3,4},{4,5},{5,6},{6,7},{8,9},{9,10},{10,11},{11... | collective-permute-start | bytes 76808 | tf_op jit(solution)/shard_map/ppermute | solution.py:18
  225.8 121.4 %copy-start.36 = (f32[8,8,128]{2,1,0:T(8,128)S(1)}, f32[8,8,128]{2,1,0:T(8,128)}, u32[]{:S(2)}) copy-start(f32[8,8,128]{2,1,0:T(8,128)} %copy-done.35) | copy-start | bytes 98308
  225.8 121.4 %copy-start.38 = (f32[8,8,128]{2,1,0:T(8,128)S(1)}, f32[8,8,128]{2,1,0:T(8,128)}, u32[]{:S(2)}) copy-start(f32[8,8,128]{2,1,0:T(8,128)} %copy-done.37) | copy-start | bytes 98308
  225.8 121.4 %copy-start.40 = (f32[8,8,128]{2,1,0:T(8,128)S(1)}, f32[8,8,128]{2,1,0:T(8,128)}, u32[]{:S(2)}) copy-start(f32[8,8,128]{2,1,0:T(8,128)} %copy-done.39) | copy-start | bytes 98308
  225.8 121.4 %copy-start.42 = (f32[8,8,128]{2,1,0:T(8,128)S(1)}, f32[8,8,128]{2,1,0:T(8,128)}, u32[]{:S(2)}) copy-start(f32[8,8,128]{2,1,0:T(8,128)} %copy-done.41) | copy-start | bytes 98308
  225.9 121.4 %copy-start.44 = (f32[8,8,128]{2,1,0:T(8,128)S(1)}, f32[8,8,128]{2,1,0:T(8,128)}, u32[]{:S(2)}) copy-start(f32[8,8,128]{2,1,0:T(8,128)} %copy-done.43) | copy-start | bytes 98308
  225.9 121.4 %copy-start.46 = (f32[8,8,128]{2,1,0:T(8,128)S(1)}, f32[8,8,128]{2,1,0:T(8,128)}, u32[]{:S(2)}) copy-start(f32[8,8,128]{2,1,0:T(8,128)} %copy-done.45) | copy-start | bytes 98308
  (98 other events, 851.2 us)
where the time goes:
time: 356 us; the launch traced here: 349 us
  blocking collectives  119 us (33%)
  starting transfers between devices  113 us (32%)
  matrix products  55.2 us (16%)
  waiting for transfers between devices  24.6 us (7%)
  other arithmetic  17.4 us (5%)
  local copies, waits for them, and re-layouts  16.3 us (5%)
    psum x1, blocking collectives, body(): closure_sum = lax.psum(grad_sum, ('gx', 'gy'))  119 us
    ppermute x18, starting transfers between devices, padded_2(): lax.ppermute(tail, axis, [(i, (i + 1) % count) for i in range(ends)])  82.5 us
    ppermute x18, starting transfers between devices, padded_2(): lax.ppermute(head, axis, [((i + 1) % count, i) for i in range(ends)])  30.2 us
    ppermute x18, waiting for transfers between devices, padded_2(): lax.ppermute(head, axis, [((i + 1) % count, i) for i in range(ends)])  21.8 us
    dot_general x8, matrix products, hidden_units(): before = jnp.einsum('hf,f...->h...', w_in, inputs, precision=PRECISE)  18.7 us
    dot_general x4, matrix products, viscosity(): logit = jnp.einsum('h,h...->...', w_out, hidden, precision=PRECISE)  8.33 us
    dot_general x4, matrix products, adjoint_step(): jnp.einsum('h...,f...->hf', before_grad, inputs, precision=PRECISE)  7.91 us
    dot_general x4, matrix products, adjoint_step(): logit = jnp.einsum('h,h...->...', w_out, hidden, precision=PRECISE)  7.21 us
  transfers between devices with their start and end apart: 36, of which 11 were waited for; matrix products, arithmetic and copies ran while one was open for 8% of the time, Pallas kernels for 0%

commit v1 on v0

--- a/solution.py
+++ b/solution.py
@@ -1,3 +1,4 @@
+import functools
 import jax
 import jax.numpy as jnp
 from jax import lax
@@ -5,6 +6,13 @@
 
 STEPS = 4
 PRECISE = lax.Precision.HIGHEST
+
+
+def produce_rates(panel, axis_name):
+    return lax.all_gather(panel, axis_name).sum(axis=0)
+
+
+derive_the_tasks = functools.partial(produce_rates, axis_name=("gx", "gy"))
 
 
 def padded_2(cells, sides, width):
@@ -160,7 +168,7 @@
             padded, viscous, fluid_padded, terrain_padded, back_padded, w_in, b_in, w_out
         )
         grad_sum = add_partial(grad_sum, partial_grad)
-    closure_sum = lax.psum(grad_sum, ("gx", "gy"))
+    closure_sum = derive_the_tasks(grad_sum)
     site_total = site_cells.shape[0] * lax.axis_size("gx") * lax.axis_size("gy")
     return (backward, closure_sum * site_total ** (-0.5))
 

time: 356 us -> 902 us (2.53)
  the two profiles are of different devices: /device:TPU:1 before, /device:TPU:128 now
where the time goes in v1:
time: 902 us; the launch traced here: 895 us
  blocking collectives  634 us (70%)
  starting transfers between devices  119 us (13%)
  matrix products  55.1 us (6%)
  waiting for transfers between devices  49.3 us (5%)
  other arithmetic  17.7 us (2%)
  local copies, waits for them, and re-layouts  16.7 us (2%)
    all_gather x1, blocking collectives, produce_rates(): return lax.all_gather(panel, axis_name).sum(axis=0)  634 us
    ppermute x18, starting transfers between devices, padded_2(): lax.ppermute(head, axis, [((i + 1) % count, i) for i in range(ends)])  59.9 us
    ppermute x18, starting transfers between devices, padded_2(): lax.ppermute(tail, axis, [(i, (i + 1) % count) for i in range(ends)])  59.2 us
    ppermute x18, waiting for transfers between devices, padded_2(): lax.ppermute(tail, axis, [(i, (i + 1) % count) for i in range(ends)])  26.3 us
    ppermute x18, waiting for transfers between devices, padded_2(): lax.ppermute(head, axis, [((i + 1) % count, i) for i in range(ends)])  23 us
    dot_general x8, matrix products, hidden_units(): before = jnp.einsum('hf,f...->h...', w_in, inputs, precision=PRECISE)  18.7 us
  transfers between devices with their start and end apart: 36, of which 17 were waited for; matrix products, arithmetic and copies ran while one was open for 3% of the time, Pallas kernels for 0%

profile of v1, /device:TPU:128, one launch (start us, length us, event | category | flops | bytes accessed | tf_op | source)
XLA Modules:
  0.0 895.2 jit_solution(306906273524392911)
XLA Ops:
  3.4 7.9 collective-permute-start.5
  13.9 7.9 collective-permute-start.1
  26.4 3.4 collective-permute-start.2
  31.1 4.2 collective-permute-done.3
  36.0 3.4 collective-permute-start.6
  40.9 4.2 collective-permute-done.7
  45.9 2.8 fusion.98
  48.7 2.1 fusion.6
  53.4 7.9 collective-permute-start.9
  62.7 4.1 collective-permute-start.10
  68.5 4.1 collective-permute-done.11
  73.3 2.8 fusion.112
  76.1 2.1 fusion.4
  79.2 1.9 collective-permute-start.12
  81.1 7.9 collective-permute-start.13
  90.5 4.0 collective-permute-start.14
  96.1 4.2 collective-permute-done.15
  100.9 2.8 fusion.110
  103.7 2.1 fusion.2
  108.2 8.3 collective-permute-start.17
  132.1 4.0 collective-permute-start.18
  137.7 4.1 collective-permute-done.19
  142.6 2.8 fusion.99
  145.4 2.1 fusion
  148.6 2.7 copy.98
  151.3 5.8 scatter_custom_fusion
  157.1 2.9 copy.99
  160.1 2.1 collective-permute-start.20
  162.1 2.4 collective-permute-start.21
  164.6 6.8 collective-permute-done.21
  172.8 4.9 collective-permute-start.23
  181.7 2.0 convolution_bitcast_fusion.3
  183.7 2.1 collective-permute-start.24
  185.8 2.4 collective-permute-start.25
  189.9 5.2 collective-permute-done.25
  196.4 4.8 collective-permute-start.27
  205.5 2.0 convolution_bitcast_fusion.2
  207.5 2.1 collective-permute-start.28
  209.6 2.4 collective-permute-start.29
  213.7 5.2 collective-permute-done.29
  220.2 5.1 collective-permute-start.31
  229.3 2.0 convolution_bitcast_fusion.1
  231.3 2.1 collective-permute-start.32
  233.4 2.4 collective-permute-start.33
  237.5 5.2 collective-permute-done.33
  244.0 6.2 collective-permute-start.35
  252.0 2.0 convolution_bitcast_fusion
  259.0 633.8 %all_gather.4 = f32[256,64,6]{1,2,0:T(8,128)S(1)} all-gather(f32[1,64,6]{1,2,0:T(8,128)S(1)} %fusion.289), channel_id=1, replica_groups=mesh['gx'=32,'gy'=8] {'gx','gy'}, dimensions={0}, use_global_device_ids=true | all-gather | bytes 394752 | tf_op jit(solution)/shard_map/all_gather | solution.py:12
  (429 shorter events, 76.6 us)
Async XLA Ops:
  0.6 45.2 %copy-start = (f32[64,4]{0,1:T(4,128)S(1)}, f32[64,4]{0,1:T(4,128)}, u32[]{:S(2)}) copy-start(f32[64,4]{0,1:T(4,128)} %param.19) | copy-start | bytes 3076
  0.6 35.2 %copy-start.7 = (f32[5,8,8,128]{3,2,1,0:T(8,128)S(1)}, f32[5,8,8,128]{3,2,1,0:T(8,128)}, u32[]{:S(2)}) copy-start(f32[5,8,8,128]{3,2,1,0:T(8,128)} %param.15) | copy-start | bytes 491524
  1.5 34.4 %collective-permute-start.4 = (f32[5,1,8,128]{3,2,1,0:T(8,128)S(1)}, f32[5,1,8,128]{3,2,1,0:T(8,128)S(1)}, u32[]{:S(2)}, u32[]{:S(2)}) collective-permute-start(f32[5,1,8,128]{3,2,1,0:T(8,128)S(1)} %get-tuple-element.168), channel_id=1, source_target_pairs={{0,8},{8,16},{16,24},{24,32},{32,40},{40,48},{48,56},{56,64},{64,7... | collective-permute-start | bytes 61448 | tf_op jit(solution)/shard_map/ppermute | solution.py:26
  3.4 32.5 %collective-permute-start.5 = (f32[5,1,8,128]{3,2,1,0:T(8,128)S(1)}, f32[5,1,8,128]{3,2,1,0:T(8,128)S(1)}, u32[]{:S(2)}, u32[]{:S(2)}) collective-permute-start(f32[5,1,8,128]{3,2,1,0:T(8,128)S(1)} %get-tuple-element.169), channel_id=1, source_target_pairs={{8,0},{16,8},{24,16},{32,24},{40,32},{48,40},{56,48},{64,56},{72,6... | collective-permute-start | bytes 61448 | tf_op jit(solution)/shard_map/ppermute | solution.py:28
  11.9 14.4 %collective-permute-start = (s32[1,8]{1,0:T(1,128)S(1)}, s32[1,8]{1,0:T(1,128)S(1)}, u32[]{:S(2)}, u32[]{:S(2)}) collective-permute-start(s32[1,8]{1,0:T(1,128)S(1)} %get-tuple-element.260), channel_id=1, source_target_pairs={{0,8},{8,16},{16,24},{24,32},{32,40},{40,48},{48,56},{56,64},{64,7... | collective-permute-start | bytes 104 | tf_op jit(solution)/shard_map/ppermute | solution.py:26
  13.9 12.4 %collective-permute-start.1 = (s32[1,8]{1,0:T(1,128)S(1)}, s32[1,8]{1,0:T(1,128)S(1)}, u32[]{:S(2)}, u32[]{:S(2)}) collective-permute-start(s32[1,8]{1,0:T(1,128)S(1)} %get-tuple-element.261), channel_id=1, source_target_pairs={{8,0},{16,8},{24,16},{32,24},{40,32},{48,40},{56,48},{64,56},{72,6... | collective-permute-start | bytes 104 | tf_op jit(solution)/shard_map/ppermute | solution.py:28
  22.8 28.2 %copy-start.8 = (f32[5,8,8,127]{3,2,1,0:T(8,128)}, f32[5,8,8,127]{3,2,1,0:T(8,128)S(1)}, u32[]{:S(2)}) copy-start(f32[5,8,8,127]{3,2,1,0:T(8,128)S(1)} %get-tuple-element.159) | copy-start | bytes 487684
  26.4 4.7 collective-permute-start.2
  29.8 5.5 collective-permute-start.3
  36.0 4.9 collective-permute-start.6
  39.4 5.7 collective-permute-start.7
  51.4 27.0 %copy-start.10 = (f32[5,8,8,127]{3,2,1,0:T(8,128)}, f32[5,8,8,127]{3,2,1,0:T(8,128)S(1)}, u32[]{:S(2)}) copy-start(f32[5,8,8,127]{3,2,1,0:T(8,128)S(1)} %get-tuple-element.154) | copy-start | bytes 487684
  51.4 27.0 %copy-start.12 = (f32[5,8,8,127]{3,2,1,0:T(8,128)}, f32[5,8,8,127]{3,2,1,0:T(8,128)S(1)}, u32[]{:S(2)}) copy-start(f32[5,8,8,127]{3,2,1,0:T(8,128)S(1)} %get-tuple-element.155) | copy-start | bytes 487684
  51.4 10.2 %collective-permute-start.8 = (f32[5,1,8,128]{3,2,1,0:T(8,128)S(1)}, f32[5,1,8,128]{3,2,1,0:T(8,128)S(1)}, u32[]{:S(2)}, u32[]{:S(2)}) collective-permute-start(f32[5,1,8,128]{3,2,1,0:T(8,128)S(1)} %get-tuple-element.156), channel_id=1, source_target_pairs={{0,8},{8,16},{16,24},{24,32},{32,40},{40,48},{48,56},{56,64},{64,7... | collective-permute-start | bytes 61448 | tf_op jit(solution)/shard_map/ppermute | solution.py:26
  53.4 9.3 %collective-permute-start.9 = (f32[5,1,8,128]{3,2,1,0:T(8,128)S(1)}, f32[5,1,8,128]{3,2,1,0:T(8,128)S(1)}, u32[]{:S(2)}, u32[]{:S(2)}) collective-permute-start(f32[5,1,8,128]{3,2,1,0:T(8,128)S(1)} %get-tuple-element.157), channel_id=1, source_target_pairs={{8,0},{16,8},{24,16},{32,24},{40,32},{48,40},{56,48},{64,56},{72,6... | collective-permute-start | bytes 61448 | tf_op jit(solution)/shard_map/ppermute | solution.py:28
  62.7 5.7 collective-permute-start.10
  66.9 5.7 collective-permute-start.11
  79.2 26.9 %copy-start.14 = (f32[5,8,8,127]{3,2,1,0:T(8,128)}, f32[5,8,8,127]{3,2,1,0:T(8,128)S(1)}, u32[]{:S(2)}) copy-start(f32[5,8,8,127]{3,2,1,0:T(8,128)S(1)} %get-tuple-element.150) | copy-start | bytes 487684
  79.2 10.2 %collective-permute-start.12 = (f32[5,1,8,128]{3,2,1,0:T(8,128)S(1)}, f32[5,1,8,128]{3,2,1,0:T(8,128)S(1)}, u32[]{:S(2)}, u32[]{:S(2)}) collective-permute-start(f32[5,1,8,128]{3,2,1,0:T(8,128)S(1)} %get-tuple-element.152), channel_id=1, source_target_pairs={{0,8},{8,16},{16,24},{24,32},{32,40},{40,48},{48,56},{56,64},{64,7... | collective-permute-start | bytes 61448 | tf_op jit(solution)/shard_map/ppermute | solution.py:26
  81.1 9.3 %collective-permute-start.13 = (f32[5,1,8,128]{3,2,1,0:T(8,128)S(1)}, f32[5,1,8,128]{3,2,1,0:T(8,128)S(1)}, u32[]{:S(2)}, u32[]{:S(2)}) collective-permute-start(f32[5,1,8,128]{3,2,1,0:T(8,128)S(1)} %get-tuple-element.153), channel_id=1, source_target_pairs={{8,0},{16,8},{24,16},{32,24},{40,32},{48,40},{56,48},{64,56},{72,6... | collective-permute-start | bytes 61448 | tf_op jit(solution)/shard_map/ppermute | solution.py:28
  90.5 5.5 collective-permute-start.14
  94.5 5.7 collective-permute-start.15
  106.3 25.7 %collective-permute-start.16 = (f32[5,1,8,128]{3,2,1,0:T(8,128)S(1)}, f32[5,1,8,128]{3,2,1,0:T(8,128)S(1)}, u32[]{:S(2)}, u32[]{:S(2)}) collective-permute-start(f32[5,1,8,128]{3,2,1,0:T(8,128)S(1)} %get-tuple-element.148), channel_id=1, source_target_pairs={{0,8},{8,16},{16,24},{24,32},{32,40},{40,48},{48,56},{56,64},{64,7... | collective-permute-start | bytes 61448 | tf_op jit(solution)/shard_map/ppermute | solution.py:26
  108.2 23.8 %collective-permute-start.17 = (f32[5,1,8,128]{3,2,1,0:T(8,128)S(1)}, f32[5,1,8,128]{3,2,1,0:T(8,128)S(1)}, u32[]{:S(2)}, u32[]{:S(2)}) collective-permute-start(f32[5,1,8,128]{3,2,1,0:T(8,128)S(1)} %get-tuple-element.149), channel_id=1, source_target_pairs={{8,0},{16,8},{24,16},{32,24},{40,32},{48,40},{56,48},{64,56},{72,6... | collective-permute-start | bytes 61448 | tf_op jit(solution)/shard_map/ppermute | solution.py:28
  132.1 5.6 collective-permute-start.18
  136.1 5.7 collective-permute-start.19
  160.1 4.6 collective-permute-start.20
  162.1 9.3 %collective-permute-start.21 = (f32[5,1,8,128]{3,2,1,0:T(8,128)S(1)}, f32[5,1,8,128]{3,2,1,0:T(8,128)S(1)}, u32[]{:S(2)}, u32[]{:S(2)}) collective-permute-start(f32[5,1,8,128]{3,2,1,0:T(8,128)S(1)} %get-tuple-element.144), channel_id=1, source_target_pairs={{0,8},{8,16},{16,24},{24,32},{32,40},{40,48},{48,56},{56,64},{64,7... | collective-permute-start | bytes 61448 | tf_op jit(solution)/shard_map/ppermute | solution.py:26
  171.5 7.4 collective-permute-start.22
  172.8 6.2 collective-permute-start.23
  183.7 6.2 collective-permute-start.24
  185.8 9.3 %collective-permute-start.25 = (f32[5,1,8,128]{3,2,1,0:T(8,128)S(1)}, f32[5,1,8,128]{3,2,1,0:T(8,128)S(1)}, u32[]{:S(2)}, u32[]{:S(2)}) collective-permute-start(f32[5,1,8,128]{3,2,1,0:T(8,128)S(1)} %get-tuple-element.137), channel_id=1, source_target_pairs={{0,8},{8,16},{16,24},{24,32},{32,40},{40,48},{48,56},{56,64},{64,7... | collective-permute-start | bytes 61448 | tf_op jit(solution)/shard_map/ppermute | solution.py:26
  195.1 6.4 collective-permute-start.26
  196.4 6.4 collective-permute-start.27
  207.5 6.2 collective-permute-start.28
  209.6 9.3 %collective-permute-start.29 = (f32[5,1,8,128]{3,2,1,0:T(8,128)S(1)}, f32[5,1,8,128]{3,2,1,0:T(8,128)S(1)}, u32[]{:S(2)}, u32[]{:S(2)}) collective-permute-start(f32[5,1,8,128]{3,2,1,0:T(8,128)S(1)} %get-tuple-element.130), channel_id=1, source_target_pairs={{0,8},{8,16},{16,24},{24,32},{32,40},{40,48},{48,56},{56,64},{64,7... | collective-permute-start | bytes 61448 | tf_op jit(solution)/shard_map/ppermute | solution.py:26
  218.9 6.6 collective-permute-start.30
  220.2 6.4 collective-permute-start.31
  231.3 6.2 collective-permute-start.32
  233.4 9.3 %collective-permute-start.33 = (f32[5,1,8,128]{3,2,1,0:T(8,128)S(1)}, f32[5,1,8,128]{3,2,1,0:T(8,128)S(1)}, u32[]{:S(2)}, u32[]{:S(2)}) collective-permute-start(f32[5,1,8,128]{3,2,1,0:T(8,128)S(1)} %get-tuple-element.123), channel_id=1, source_target_pairs={{0,8},{8,16},{16,24},{24,32},{32,40},{40,48},{48,56},{56,64},{64,7... | collective-permute-start | bytes 61448 | tf_op jit(solution)/shard_map/ppermute | solution.py:26
  242.7 7.7 collective-permute-start.34
  244.0 7.7 collective-permute-start.35
  257.2 636.6 %copy-start.36 = (f32[8,8,128]{2,1,0:T(8,128)S(1)}, f32[8,8,128]{2,1,0:T(8,128)}, u32[]{:S(2)}) copy-start(f32[8,8,128]{2,1,0:T(8,128)} %copy-done.35) | copy-start | bytes 98308
  257.2 636.6 %copy-start.38 = (f32[8,8,128]{2,1,0:T(8,128)S(1)}, f32[8,8,128]{2,1,0:T(8,128)}, u32[]{:S(2)}) copy-start(f32[8,8,128]{2,1,0:T(8,128)} %copy-done.37) | copy-start | bytes 98308
  257.2 636.6 %copy-start.40 = (f32[8,8,128]{2,1,0:T(8,128)S(1)}, f32[8,8,128]{2,1,0:T(8,128)}, u32[]{:S(2)}) copy-start(f32[8,8,128]{2,1,0:T(8,128)} %copy-done.39) | copy-start | bytes 98308
  257.2 636.6 %copy-start.42 = (f32[8,8,128]{2,1,0:T(8,128)S(1)}, f32[8,8,128]{2,1,0:T(8,128)}, u32[]{:S(2)}) copy-start(f32[8,8,128]{2,1,0:T(8,128)} %copy-done.41) | copy-start | bytes 98308
  257.2 636.6 %copy-start.44 = (f32[8,8,128]{2,1,0:T(8,128)S(1)}, f32[8,8,128]{2,1,0:T(8,128)}, u32[]{:S(2)}) copy-start(f32[8,8,128]{2,1,0:T(8,128)} %copy-done.43) | copy-start | bytes 98308
  257.2 636.6 %copy-start.46 = (f32[8,8,128]{2,1,0:T(8,128)S(1)}, f32[8,8,128]{2,1,0:T(8,128)}, u32[]{:S(2)}) copy-start(f32[8,8,128]{2,1,0:T(8,128)} %copy-done.45) | copy-start | bytes 98308
  (98 other events, 975.1 us)
